TPU v7x, 512 devices: a whole 4x4x16 slice. The times are simulated.
512 devices in a mesh: tm: 32 (over z, x_lo), recv: 16 (over x_hi, y, core).
Axes of the slice: x: 4 (x_hi: 2, x_lo: 2; x = x_hi * 2 + x_lo), y: 4, z: 16, core: 2. Of those that a mesh axis runs over, the one named last changes fastest.
Arguments:
- traces: bfloat16 [128, 4096, 2048], P('tm', 'recv'), may hold values from -6 to 6
- valid: int32 [128, 4096], P('tm', 'recv'), may hold values 0 or 1
- src_idx: int32 [32], replicated, may hold values from 0 to 4095
Outputs:
- stacks: float32 [32, 2, 61, 4096], P('tm', None, None, 'recv')
All inputs are finite; a program needn't handle non-finite values. No bound on the sum of `valid` on one device may be relied on, other than what follows from the above.
Results may differ from a plain program's by a relative error of at most 0.0035.
Values sent between devices are 32-bit elements; how exact they have to be, the bound alone decides.
No kernel may reach another device: no remote copies, remote signals or barrier semaphores. Data moves between devices by JAX's collectives and lax.ppermute only.
A program may use at most 64 MiB of HBM per device.

v0:
```python
import math
import jax
import jax.numpy as jnp
from jax import lax
from jax.sharding import PartitionSpec as P

NS = 2048
NB = 61
BIN0 = 40


def basis_table():
    sample_ids = jnp.arange(NS, dtype=jnp.int32)
    bin_ids = BIN0 + jnp.arange(NB, dtype=jnp.int32)
    phase_ids = bin_ids[:, None] * sample_ids[None, :] % NS
    angle = 2.0 * math.pi / NS * phase_ids.astype(jnp.float32)
    return jnp.concatenate([jnp.cos(angle), -jnp.sin(angle)], axis=0).astype(jnp.bfloat16)


def whiten_block(spec, valid_float):
    real_part = spec[:NB]
    imag_part = spec[NB:]
    power = real_part * real_part + imag_part * imag_part
    level = jnp.sum(power, axis=0) / (2.0 * NB)
    scale = lax.rsqrt(power + level[None] + 1e-06) * valid_float[None]
    return jnp.concatenate([real_part * scale, imag_part * scale], axis=0)


def share_panel(partial_value):
    return lax.psum(partial_value, "recv")


def cross_terms(panel, white, factor):
    high = lax.Precision.HIGHEST
    src_real = panel[:NB]
    src_imag = panel[NB:]
    own_real = white[:NB]
    own_imag = white[NB:]
    real_sum = jnp.einsum("fts,ftc->sfc", src_real, own_real, precision=high) + jnp.einsum(
        "fts,ftc->sfc", src_imag, own_imag, precision=high
    )
    imag_sum = jnp.einsum("fts,ftc->sfc", src_real, own_imag, precision=high) - jnp.einsum(
        "fts,ftc->sfc", src_imag, own_real, precision=high
    )
    return jnp.stack([real_sum, imag_sum], axis=1) * factor


def on_device(traces, valid, src_idx):
    seg_count = traces.shape[0]
    chan_count = traces.shape[1]
    basis = basis_table()
    valid_float = valid.astype(jnp.float32)
    offset = lax.axis_index("recv") * chan_count
    onehot = (src_idx[:, None] == offset + jnp.arange(chan_count, dtype=jnp.int32)[None, :]).astype(
        jnp.float32
    )
    spec = lax.dot_general(
        basis, traces, (((1,), (2,)), ((), ())), preferred_element_type=jnp.float32
    )
    white = whiten_block(spec, valid_float)
    partial_value = jnp.einsum("ktc,sc->kts", white, onehot, precision=lax.Precision.HIGHEST)
    panel = share_panel(partial_value)
    factor = 1.0 / math.sqrt(seg_count * lax.axis_size("tm"))
    totals = cross_terms(panel, white, factor)
    return lax.psum_scatter(totals, "tm", scatter_dimension=0, tiled=True)


def solution(mesh):
    return jax.shard_map(
        on_device,
        mesh=mesh,
        in_specs=(P("tm", "recv", None), P("tm", "recv"), P()),
        out_specs=P("tm", None, None, "recv"),
        check_vma=False,
    )
```

profile of v0, /device:TPU:2, one launch (start us, length us, event | category | flops | bytes accessed | tf_op | source)
XLA Modules:
  0.0 392.3 jit_solution(107525465795028076)
XLA Ops:
  6.5 0.0 all-reduce.3.cloned.1.call-start
  6.5 2.4 cosine_convert_fusion
  9.0 0.0 copy-start
  9.0 0.0 copy-start.1
  9.0 3.7 fusion.3
  12.7 0.1 fusion.25
  12.8 0.0 copy-done
  12.9 0.1 slice_multiply_fusion.1
  13.0 0.0 copy-done.1
  13.0 0.4 fusion.6
  13.4 68.9 %psum.7 = f32[122,4,32]{0,2,1:T(8,128)S(1)} all-reduce(f32[122,4,32]{0,2,1:T(8,128)S(1)} %fusion.6), channel_id=1, replica_groups=mesh['tm'=32,'recv'=16] {'recv'}, use_global_device_ids=true, to_apply=%region_1.2 | all-reduce | flops 15616 | bytes 124928 | tf_op jit(solution)/shard_map/psum | solution.py:30
  82.3 0.1 fusion.26
  82.4 0.1 copy.14
  82.5 3.1 fusion.17
  85.6 1.8 fusion.13
  87.4 0.1 copy.16
  87.5 3.3 add_bitcast_fusion
  90.8 1.8 subtract_bitcast_fusion
  92.6 0.5 maximum_multiply_fusion
  93.1 5.0 %copy.21 = f32[32,2,61,256]{3,1,2,0:T(2,128)} copy(f32[32,2,61,256]{3,0,2,1:T(8,128)S(1)} %maximum_multiply_fusion) | data formatting | bytes 7995392 | tf_op jit(solution)/shard_map/mul | solution.py:45
  98.1 0.0 all-reduce.3.cloned.1.call-update
  98.1 1.2 dynamic-slice
  99.3 284.0 %all-reduce.3.cloned.1.call-done = f32[32,2,61,256]{3,1,2,0:T(2,128)} async-done(((f32[32,2,61,256]{3,1,2,0:T(2,128)}), f32[32,2,61,256]{3,1,2,0:T(2,128)}) %all-reduce.3.cloned.1.call-update) | async-done | bytes 3997712
  383.4 2.1 constant_dynamic-slice_fusion
  (4 shorter events, 0.0 us)
Async XLA Ops:
  6.5 376.8 %all-reduce.3.cloned.1.call-start = ((), (), s32[]{:S(2)}) async-start(), calls=%async_computation | async-start | bytes 7995392
  9.0 3.8 copy-start
  9.0 4.0 %copy-start.1 = (s32[32]{0:T(128)S(1)}, s32[32]{0:T(128)}, u32[]{:S(2)}) copy-start(s32[32]{0:T(128)} %param.5) | copy-start | bytes 388
Sparse Core Ops, SparseCore 0:
  98.2 285.1 all-reduce.2
where the time goes:
time: 393 us; the launch traced here: 392 us
  waiting for transfers between devices  284 us (72%)
  blocking collectives  68.9 us (18%)
  matrix products  14.1 us (4%)
  between operations  13.5 us (3%)
  local copies, waits for them, and re-layouts  8.66 us (2%)
    unnamed x2, waiting for transfers between devices  284 us
    psum x1, blocking collectives, share_panel(): return lax.psum(partial_value, 'recv')  68.9 us
  transfers between devices with their start and end apart: 1, of which 1 were waited for; matrix products, arithmetic and copies ran while one was open for 0% of the time, Pallas kernels for 0%

commit v1 on v0

--- a/solution.py
+++ b/solution.py
@@ -27,7 +27,7 @@
 
 
 def share_panel(partial_value):
-    return lax.psum(partial_value, "recv")
+    return jnp.sum(lax.all_gather(partial_value, "recv"), axis=0)
 
 
 def cross_terms(panel, white, factor):

time: 393 us -> 362 us (0.921)
  blocking collectives: 68.9 us -> 38.9 us
    psum x1 -> x0, blocking collectives: 68.9 us -> none  [share_panel(): return lax.psum(partial_value, 'recv')]
    all_gather x0 -> x1, blocking collectives: none -> 38.9 us  [share_panel(): return jnp.sum(lax.all_gather(partial_value, 'recv'), axis=0)]
where the time goes in v1:
time: 362 us
  waiting for transfers between devices  283 us (78%)
  blocking collectives  38.9 us (11%)
  between operations  13.5 us (4%)
  matrix products  11.2 us (3%)
  local copies, waits for them, and re-layouts  8.49 us (2%)
  other arithmetic  6.11 us (2%)
    unnamed x2, waiting for transfers between devices  283 us
    all_gather x1, blocking collectives, share_panel(): return jnp.sum(lax.all_gather(partial_value, 'recv'), axis=0)  38.9 us
  transfers between devices with their start and end apart: 1, of which 1 were waited for; matrix products, arithmetic and copies ran while one was open for 0% of the time, Pallas kernels for 0%

profile of v1, /device:TPU:2, one launch (start us, length us, event | category | flops | bytes accessed | tf_op | source)
XLA Modules:
  0.0 361.6 jit_solution(8717010030322363761)
XLA Ops:
  6.5 0.0 copy-start
  6.5 0.0 copy-start.1
  6.5 0.0 all-reduce.3.cloned.1.call-start
  6.6 2.5 cosine_convert_fusion
  9.0 3.7 %fusion.3 = f32[122,4,256]{2,0,1:T(8,128)S(1)} fusion(bf16[4,256,2048]{2,1,0:T(8,128)(2,1)} %param.3, bf16[61,2048]{1,0:T(8,128)(2,1)S(1)} %get-tuple-element.8, bf16[61,2048]{1,0:T(8,128)(2,1)S(1)} %get-tuple-element.7), kind=kOutput, calls=%fused_computation.10 | convolution fusion | flops 512704512 | bytes 5193728 | tf_op jit(solution)/shard_map/dot_general | solution.py:57
  12.7 0.1 fusion.29
  12.8 0.0 copy-done
  12.8 0.1 slice_multiply_fusion.1
  13.0 0.0 copy-done.1
  13.0 0.4 fusion.6
  13.4 0.2 copy.9
  13.5 38.9 %all-gather = f32[1952,4,32]{2,1,0:T(4,128)} all-gather(f32[122,4,32]{2,1,0:T(4,128)S(1)} %copy.9), channel_id=2, replica_groups=mesh['tm'=32,'recv'=16] {'recv'}, dimensions={0}, use_global_device_ids=true | all-gather | bytes 1061888 | tf_op jit(solution)/shard_map/all_gather | solution.py:30
  52.4 3.0 reduce_sum.19
  55.4 1.8 fusion.17
  57.2 1.8 fusion.13
  59.0 1.8 add_bitcast_fusion
  60.8 1.8 subtract_bitcast_fusion
  62.6 0.5 maximum_multiply_fusion
  63.1 5.0 %copy.17 = f32[32,2,61,256]{3,1,2,0:T(2,128)} copy(f32[32,2,61,256]{3,0,2,1:T(8,128)S(1)} %maximum_multiply_fusion) | data formatting | bytes 7995392 | tf_op jit(solution)/shard_map/mul | solution.py:45
  68.0 0.0 all-reduce.3.cloned.1.call-update
  68.1 1.2 dynamic-slice
  69.3 283.4 %all-reduce.3.cloned.1.call-done = f32[32,2,61,256]{3,1,2,0:T(2,128)} async-done(((f32[32,2,61,256]{3,1,2,0:T(2,128)}), f32[32,2,61,256]{3,1,2,0:T(2,128)}) %all-reduce.3.cloned.1.call-update) | async-done | bytes 3997712
  352.7 2.1 constant_dynamic-slice_fusion
  (4 shorter events, 0.0 us)
Async XLA Ops:
  6.5 6.3 %copy-start = (s32[4,256]{1,0:T(4,128)S(1)}, s32[4,256]{1,0:T(4,128)}, u32[]{:S(2)}) copy-start(s32[4,256]{1,0:T(4,128)} %param.4) | copy-start | bytes 12292
  6.5 6.4 %copy-start.1 = (s32[32]{0:T(128)S(1)}, s32[32]{0:T(128)}, u32[]{:S(2)}) copy-start(s32[32]{0:T(128)} %param.5) | copy-start | bytes 388
  6.5 346.1 %all-reduce.3.cloned.1.call-start = ((), (), s32[]{:S(2)}) async-start(), calls=%async_computation | async-start | bytes 7995392
Sparse Core Ops, SparseCore 0:
  68.2 284.4 all-reduce.2
